TPU v7x, 256 devices: a whole 4x4x8 slice. The times are simulated.
256 devices in a mesh: dp: 2 (over z_lo), expert: 32 (over y, z_hi, core), tensor: 4 (over x).
Axes of the slice: x: 4, y: 4, z: 8 (z_hi: 4, z_lo: 2; z = z_hi * 2 + z_lo), core: 2. Of those that a mesh axis runs over, the one named last changes fastest.
Arguments:
- context: bfloat16 [8192, 2048], P(('dp', 'expert'), 'tensor'), may hold values from -6 to 6
- residual: bfloat16 [8192, 2048], P(('dp', 'expert')), may hold values from -6 to 6
- wo_rows: bfloat16 [2048, 2048], P('tensor'), may hold values from -0.125 to 0.125
- norm_gain: float32 [2048], replicated, may hold values from 0.25 to 1.75
- analyzer_out: bfloat16 [8192, 2048], P(('dp', 'expert'), 'tensor'), may hold values from -6 to 6
- gate_probs: float32 [8192, 6], P(('dp', 'expert')), may hold values from 0.05 to 0.5
- expert_ids: int32 [8192, 6], P(('dp', 'expert')), may hold values from 0 to 63, all different within a row; in each aligned block of 128 rows (0 to 127, 128 to 255, ...) at most 14 rows name the same one
- w_gate_up: bfloat16 [64, 2, 2048, 1408], P('expert', None, 'dp', 'tensor'), may hold values from -0.125 to 0.125
- w_down: bfloat16 [64, 1408, 2048], P('expert', 'tensor', 'dp'), may hold values from -0.15625 to 0.15625
Outputs:
- block_out: bfloat16 [8192, 2048], P(('dp', 'expert'), 'tensor')
- context_grad: bfloat16 [8192, 2048], P(('dp', 'expert'), 'tensor')
- gate_prob_grad: float32 [8192, 6], P(('dp', 'expert'))
- gate_up_grad: bfloat16 [64, 2, 2048, 1408], P('expert', None, 'dp', 'tensor')
- down_grad: bfloat16 [64, 1408, 2048], P('expert', 'tensor', 'dp')
Inputs may be any that keep to these rules, and one draw needn't show every extreme that they name: `expert_ids`: each row names 6 different experts; within each device's rows (aligned blocks of 128 rows) no expert is named more than 14 times, a bound that some block reaches.
All inputs are finite; a program needn't handle non-finite values.
Results may differ from a plain program's by a relative error of at most 0.024.
Values may be sent and summed in bfloat16 or wider, within the bound.
No kernel may reach another device: no remote copies, remote signals or barrier semaphores. Data moves between devices by JAX's collectives and lax.ppermute only.
A program may use at most 128 MiB of HBM per device.

v0:
```python
import jax
import jax.numpy as jnp
from jax import lax
from jax.sharding import PartitionSpec as P

EXPERTS = 64
CAP = 14
NORM_EPS = 1e-06
LOSS_WEIGHT = 0.25


def to_experts(outgoing):
    return lax.all_to_all(outgoing, "expert", split_axis=1, concat_axis=1, tiled=True)


def to_tokens(outgoing):
    return lax.all_to_all(outgoing, "expert", split_axis=1, concat_axis=1, tiled=True)


def weight_terms(arrived, activation, grad_in, d_gate_pre, d_up_pre):
    down_part = jnp.einsum(
        "escf,escd->efd", activation, grad_in, preferred_element_type=jnp.float32
    )
    gate_part = jnp.einsum(
        "escd,escf->edf", arrived, d_gate_pre, preferred_element_type=jnp.float32
    )
    up_part = jnp.einsum("escd,escf->edf", arrived, d_up_pre, preferred_element_type=jnp.float32)
    return (jnp.stack([gate_part, up_part], axis=1), down_part)


def per_device(
    context, residual, wo_rows, norm_gain, analyzer_out, gate_probs, expert_ids, w_gate_up, w_down
):
    tok_count, top_count = expert_ids.shape
    feature_count = residual.shape[1]
    tensor_count = lax.axis_size("tensor")
    expert_ranks = lax.axis_size("expert")
    col_count = feature_count // tensor_count
    col_start = lax.axis_index("tensor") * col_count
    local_experts = w_gate_up.shape[0]
    slot_count = EXPERTS * CAP
    expert_range = jnp.arange(EXPERTS, dtype=jnp.int32)
    slot_order = expert_range % local_experts * expert_ranks + expert_range // local_experts
    gate_up_full, down_full = (
        lax.all_gather(w_gate_up, "dp", axis=2, tiled=True),
        lax.all_gather(w_down, "dp", axis=2, tiled=True),
    )
    partial_attn = jnp.dot(context, wo_rows, preferred_element_type=jnp.float32)
    hidden_in = residual.astype(jnp.float32) + lax.psum(
        partial_attn.astype(jnp.bfloat16), "tensor"
    ).astype(jnp.float32)
    inv_rms = lax.rsqrt(jnp.mean(hidden_in * hidden_in, axis=1, keepdims=True) + NORM_EPS)
    normed = (norm_gain * hidden_in * inv_rms).astype(jnp.bfloat16)
    flat_ids = expert_ids.reshape(-1)
    onehot = (flat_ids[:, None] == expert_range[None, :]).astype(jnp.int32)
    slot_index = jnp.sum((jnp.cumsum(onehot, axis=0) - onehot) * onehot, axis=1)
    expert_slot = jnp.sum(onehot * slot_order[None, :], axis=1)
    dest_row = expert_slot * CAP + slot_index
    sentinel = tok_count * top_count
    row_entry = (
        jnp.full((slot_count,), sentinel, jnp.int32)
        .at[dest_row]
        .set(jnp.arange(sentinel, dtype=jnp.int32))
    )
    row_token = row_entry // top_count
    gate_pad = jnp.concatenate([gate_probs.reshape(-1), jnp.zeros((1,), jnp.float32)])
    row_gate = gate_pad[row_entry]
    normed_pad = jnp.concatenate([normed, jnp.zeros((1, feature_count), jnp.bfloat16)], axis=0)
    outgoing = normed_pad[row_token].reshape(local_experts, expert_ranks, CAP, feature_count)
    arrived = to_experts(outgoing)
    gate_full = gate_up_full[:, 0]
    up_full = gate_up_full[:, 1]
    pre_gate = jnp.einsum("escd,edf->escf", arrived, gate_full, preferred_element_type=jnp.float32)
    pre_up = jnp.einsum("escd,edf->escf", arrived, up_full, preferred_element_type=jnp.float32)
    activation = (jax.nn.silu(pre_gate) * pre_up).astype(jnp.bfloat16)
    partial_out = jnp.einsum(
        "escf,efd->escd", activation, down_full, preferred_element_type=jnp.float32
    )
    summed_out = lax.psum_scatter(
        partial_out.astype(jnp.bfloat16), "tensor", scatter_dimension=3, tiled=True
    )
    returned = to_tokens(summed_out).reshape(slot_count, col_count)
    entry_out = returned[dest_row].reshape(tok_count, top_count, col_count).astype(jnp.float32)
    hidden_cols = lax.dynamic_slice_in_dim(hidden_in, col_start, col_count, 1)
    block_out = (hidden_cols + jnp.sum(gate_probs[:, :, None] * entry_out, axis=1)).astype(
        jnp.bfloat16
    )
    error = (
        LOSS_WEIGHT * (block_out.astype(jnp.float32) - analyzer_out.astype(jnp.float32))
    ).astype(jnp.bfloat16)
    gate_partial = jnp.sum(error.astype(jnp.float32)[:, None, :] * entry_out, axis=2)
    error_full = lax.all_gather(error, "tensor", axis=1, tiled=True)
    error_pad = jnp.concatenate([error_full, jnp.zeros((1, feature_count), jnp.bfloat16)], axis=0)
    grad_slot = (row_gate[:, None] * error_pad[row_token].astype(jnp.float32)).astype(jnp.bfloat16)
    grad_slot = grad_slot.reshape(local_experts, expert_ranks, CAP, feature_count)
    grad_in = to_experts(grad_slot)
    d_act = jnp.einsum("escd,efd->escf", grad_in, down_full, preferred_element_type=jnp.float32)
    sigmoid_pre = jax.nn.sigmoid(pre_gate)
    d_gate_pre = (d_act * pre_up * sigmoid_pre * (1.0 + pre_gate * (1.0 - sigmoid_pre))).astype(
        jnp.bfloat16
    )
    d_up_pre = (d_act * pre_gate * sigmoid_pre).astype(jnp.bfloat16)
    d_entry_part = jnp.einsum(
        "escf,edf->escd", d_gate_pre, gate_full, preferred_element_type=jnp.float32
    )
    d_entry_part = d_entry_part + jnp.einsum(
        "escf,edf->escd", d_up_pre, up_full, preferred_element_type=jnp.float32
    )
    d_entry_sum = lax.psum_scatter(
        d_entry_part.astype(jnp.bfloat16), "tensor", scatter_dimension=3, tiled=True
    )
    d_returned = to_tokens(d_entry_sum).reshape(slot_count, col_count)
    d_normed = jnp.sum(
        d_returned[dest_row].reshape(tok_count, top_count, col_count).astype(jnp.float32), axis=1
    )
    gain_cols = lax.dynamic_slice_in_dim(norm_gain, col_start, col_count, 0)
    scaled = gain_cols * d_normed
    norm_partial = jnp.sum(scaled * hidden_cols, axis=1)
    norm_dots, gate_prob_grad = lax.psum((norm_partial, gate_partial), "tensor")
    cubed = inv_rms * inv_rms * inv_rms
    d_hidden = (
        error.astype(jnp.float32)
        + inv_rms * scaled
        - hidden_cols * cubed * norm_dots[:, None] / feature_count
    ).astype(jnp.bfloat16)
    context_grad = lax.dot_general(
        lax.all_gather(d_hidden, "tensor", axis=1, tiled=True),
        wo_rows,
        (((1,), (1,)), ((), ())),
        preferred_element_type=jnp.float32,
    ).astype(jnp.bfloat16)
    gate_up_part, down_part = weight_terms(arrived, activation, grad_in, d_gate_pre, d_up_pre)
    gate_up_grad, down_grad = (
        lax.psum_scatter(
            gate_up_part.astype(jnp.bfloat16), "dp", scatter_dimension=2, tiled=True
        ).astype(jnp.float32),
        lax.psum_scatter(
            down_part.astype(jnp.bfloat16), "dp", scatter_dimension=2, tiled=True
        ).astype(jnp.float32),
    )
    return (
        block_out,
        context_grad,
        gate_prob_grad,
        gate_up_grad.astype(jnp.bfloat16),
        down_grad.astype(jnp.bfloat16),
    )


def solution(mesh):
    in_specs = (
        P(("dp", "expert"), "tensor"),
        P(("dp", "expert"), None),
        P("tensor", None),
        P(),
        P(("dp", "expert"), "tensor"),
        P(("dp", "expert"), None),
        P(("dp", "expert"), None),
        P("expert", None, "dp", "tensor"),
        P("expert", "tensor", "dp"),
    )
    out_specs = (
        P(("dp", "expert"), "tensor"),
        P(("dp", "expert"), "tensor"),
        P(("dp", "expert"), None),
        P("expert", None, "dp", "tensor"),
        P("expert", "tensor", "dp"),
    )
    return jax.shard_map(
        per_device, mesh=mesh, in_specs=in_specs, out_specs=out_specs, check_vma=False
    )
```

profile of v0, /device:TPU:1, one launch (start us, length us, event | category | flops | bytes accessed | tf_op | source)
XLA Modules:
  0.0 653.3 jit_solution(14605199587444355152)
XLA Ops:
  22.3 39.6 %all-reduce.5.cloned.1.call-done = bf16[128,2048]{1,0:T(8,128)(2,1)} async-done(((bf16[128,2048]{1,0:T(8,128)(2,1)}), bf16[128,2048]{1,0:T(8,128)(2,1)}) %all-reduce.5.cloned.1.call-update) | async-done | bytes 524304 | tf_op jit(solution)/shard_map/psum | solution.py:49
  70.5 6.0 reshape.133
  76.5 7.8 %copy.53 = bf16[2,32,14,2048]{3,0,2,1:T(2,128)(2,1)} copy(bf16[2,32,14,2048]{3,2,1,0:T(8,128)(2,1)} %reshape.133) | data formatting | bytes 7340032 | tf_op jit(solution)/shard_map/reshape | solution.py:69
  84.3 12.4 %all-to-all-start = ((bf16[2,32,14,2048]{3,0,2,1:T(2,128)(2,1)}), bf16[2,32,14,2048]{3,0,2,1:T(2,128)(2,1)}, u32[]{:S(2)}, u32[]{:S(2)}) async-start(bf16[2,32,14,2048]{3,0,2,1:T(2,128)(2,1)} %copy.53), calls=%async_computation | async-start | bytes 7340032 | tf_op jit(solution)/shard_map/all_to_all | solution.py:13
  98.7 109.8 %all-to-all-done = bf16[2,32,14,2048]{3,0,2,1:T(2,128)(2,1)} async-done(((bf16[2,32,14,2048]{3,0,2,1:T(2,128)(2,1)}), bf16[2,32,14,2048]{3,0,2,1:T(2,128)(2,1)}, u32[]{:S(2)}, u32[]{:S(2)}) %all-to-all-start) | async-done | bytes 3670048 | tf_op jit(solution)/shard_map/all_to_all | solution.py:13
  208.5 7.4 %fusion.8 = f32[2,32,14,352]{3,1,2,0:T(8,128)S(1)} fusion(bf16[2,2,2048,352]{2,3,0,1:T(8,128)(2,1)} %all-gather.3.cloned.1.call-done, bf16[2,32,14,2048]{3,0,2,1:T(2,128)(2,1)} %all-to-all-done), kind=kOutput, calls=%fused_computation.23 | convolution fusion | flops 1291845632 | bytes 7815168 | tf_op jit(solution)/shard_map/escd,edf->escf/dot_general | solution.py:73
  217.1 7.7 %multiply_convert_fusion.3 = (bf16[2,32,14,352]{3,1,2,0:T(8,128)(2,1)S(1)}, f32[2,32,14,352]{3,1,2,0:T(8,128)}) fusion(f32[2,32,14,352]{3,1,2,0:T(8,128)S(1)} %fusion.8, bf16[2,2,2048,352]{2,3,0,1:T(8,128)(2,1)S(1)} %copy-done.1, bf16[2,32,14,2048]{3,0,2,1:T(2,128)(2,1)} %all-to-all-done), kind=kOutput, calls=%fused_computation.34 | convolution fusion | flops 1293737984 | bytes 9822208 | tf_op jit(solution)/shard_map/escd,edf->escf/dot_general | solution.py:74
  230.8 41.4 %reduce-scatter.5.cloned.1.call-done = bf16[2,32,14,512]{3,1,2,0:T(8,128)(2,1)} async-done(((bf16[2,32,14,2048]{3,1,2,0:T(8,128)(2,1)}), bf16[2,32,14,512]{3,1,2,0:T(8,128)(2,1)}) %reduce-scatter.5.cloned.1.call-update) | async-done | bytes 917520 | tf_op jit(solution)/shard_map/reduce_scatter | solution.py:79
  275.2 10.7 %all-to-all-start.1 = ((bf16[2,32,14,512]{3,0,2,1:T(2,128)(2,1)}), bf16[2,32,14,512]{3,0,2,1:T(2,128)(2,1)S(1)}, u32[]{:S(2)}, u32[]{:S(2)}) async-start(bf16[2,32,14,512]{3,0,2,1:T(2,128)(2,1)} %copy.57), calls=%async_computation.2 | async-start | bytes 1835008 | tf_op jit(solution)/shard_map/all_to_all | solution.py:17
  290.1 21.6 %all-to-all-done.1 = bf16[2,32,14,512]{3,0,2,1:T(2,128)(2,1)S(1)} async-done(((bf16[2,32,14,512]{3,0,2,1:T(2,128)(2,1)}), bf16[2,32,14,512]{3,0,2,1:T(2,128)(2,1)S(1)}, u32[]{:S(2)}, u32[]{:S(2)}) %all-to-all-start.1) | async-done | bytes 917536 | tf_op jit(solution)/shard_map/all_to_all | solution.py:17
  324.2 10.3 %all_gather.14 = bf16[128,2048]{1,0:T(8,128)(2,1)S(1)} all-gather(bf16[128,512]{1,0:T(8,128)(2,1)S(1)} %get-tuple-element.30), channel_id=1, replica_groups=mesh['dp'=2,'expert'=32,'tensor'=4] {'tensor'}, dimensions={1}, use_global_device_ids=true | all-gather | bytes 655360 | tf_op jit(solution)/shard_map/all_gather | solution.py:92
  339.5 6.3 reshape.138
  353.5 92.5 %all_to_all.20 = bf16[2,32,14,2048]{3,0,2,1:T(2,128)(2,1)S(1)} all-to-all(bf16[2,32,14,2048]{3,0,2,1:T(2,128)(2,1)S(1)} %copy.60), channel_id=1, replica_groups=mesh['dp'=2,'expert'=32,'tensor'=4] {'expert'}, dimensions={1} | all-to-all | bytes 7340032 | tf_op jit(solution)/shard_map/all_to_all | solution.py:13
  446.0 7.9 %multiply_convert_fusion.1 = (bf16[2,32,14,352]{3,1,2,0:T(8,128)(2,1)S(1)}, bf16[2,32,14,352]{3,1,2,0:T(8,128)(2,1)S(1)}) fusion(f32[2,32,14,352]{3,1,2,0:T(8,128)} %copy-done.14, f32[2,32,14,352]{3,1,2,0:T(8,128)} %get-tuple-element.41, bf16[2,352,2048]{2,1,0:T(8,128)(2,1)S(1)} %copy-done.4, bf16[2,32,14,2048]{3,0,2,1:T(2,128)(2,1)S(1)} %all_to_all.20), kind=kOutput, calls=%fused_computation.32 | convolution fusion | flops 1295945728 | bytes 10338304 | tf_op jit(solution)/shard_map/escd,efd->escf/dot_general | solution.py:97
  460.3 6.8 %fusion.4 = bf16[2,1,2048,352]{2,3,0,1:T(8,128)(2,1)S(1)} fusion(bf16[2,32,14,352]{3,1,2,0:T(8,128)(2,1)S(1)} %get-tuple-element.32, bf16[2,32,14,2048]{3,0,2,1:T(2,128)(2,1)} %all-to-all-done), kind=kOutput, calls=%fused_computation.17 | convolution fusion | flops 1293287424 | bytes 7184384 | tf_op jit(solution)/shard_map/escd,escf->edf/dot_general | solution.py:27
  467.2 6.8 %fusion.3 = bf16[2,1,2048,352]{2,3,0,1:T(8,128)(2,1)S(1)} fusion(bf16[2,32,14,352]{3,1,2,0:T(8,128)(2,1)S(1)} %copy-done.9, bf16[2,32,14,2048]{3,0,2,1:T(2,128)(2,1)} %all-to-all-done), kind=kOutput, calls=%fused_computation.16 | convolution fusion | flops 1293287424 | bytes 7184384 | tf_op jit(solution)/shard_map/escd,escf->edf/dot_general | solution.py:24
  478.1 8.3 %bitcast_convert_fusion = bf16[2,352,2048]{2,1,0:T(8,128)(2,1)} fusion(bf16[2,32,14,352]{3,1,2,0:T(8,128)(2,1)S(1)} %copy-done.7, bf16[2,32,14,2048]{3,0,2,1:T(2,128)(2,1)} %copy-done.2), kind=kOutput, calls=%fused_computation.9 | convolution fusion | flops 1293287424 | bytes 7184384 | tf_op jit(solution)/shard_map/escf,escd->efd/dot_general | solution.py:21
  486.4 13.3 %reduce-scatter.7.cloned.1.call-done = bf16[2,32,14,512]{3,1,2,0:T(8,128)(2,1)} async-done(((bf16[2,32,14,2048]{3,1,2,0:T(8,128)(2,1)}), bf16[2,32,14,512]{3,1,2,0:T(8,128)(2,1)}) %reduce-scatter.7.cloned.1.call-update) | async-done | bytes 917520 | tf_op jit(solution)/shard_map/reduce_scatter | solution.py:109
  502.8 10.3 %all-to-all-start.3 = ((bf16[2,32,14,512]{3,0,2,1:T(2,128)(2,1)}), bf16[2,32,14,512]{3,0,2,1:T(2,128)(2,1)S(1)}, u32[]{:S(2)}, u32[]{:S(2)}) async-start(bf16[2,32,14,512]{3,0,2,1:T(2,128)(2,1)} %copy.62), calls=%async_computation.5 | async-start | bytes 1835008 | tf_op jit(solution)/shard_map/all_to_all | solution.py:17
  516.3 33.2 %all-to-all-done.3 = bf16[2,32,14,512]{3,0,2,1:T(2,128)(2,1)S(1)} async-done(((bf16[2,32,14,512]{3,0,2,1:T(2,128)(2,1)}), bf16[2,32,14,512]{3,0,2,1:T(2,128)(2,1)S(1)}, u32[]{:S(2)}, u32[]{:S(2)}) %all-to-all-start.3) | async-done | bytes 917536 | tf_op jit(solution)/shard_map/all_to_all | solution.py:17
  560.7 12.6 %all-reduce.2 = (f32[128]{0:T(128)}, f32[128,6]{1,0:T(8,128)}) all-reduce(f32[128]{0:T(128)S(1)} %multiply_reduce_fusion.3, f32[128,6]{1,0:T(8,128)} %multiply_reduce_fusion), channel_id=1, replica_groups=mesh['dp'=2,'expert'=32,'tensor'=4] {'tensor'}, use_global_device_ids=true, to_apply=%region_12.13 | all-reduce | flops 896 | bytes 7168 | tf_op jit(solution)/shard_map/psum | solution.py:119
  575.6 10.6 %all_gather.15 = bf16[128,2048]{1,0:T(8,128)(2,1)S(1)} all-gather(bf16[128,512]{1,0:T(8,128)(2,1)S(1)} %subtract_convert_fusion), channel_id=1, replica_groups=mesh['dp'=2,'expert'=32,'tensor'=4] {'tensor'}, dimensions={1}, use_global_device_ids=true | all-gather | bytes 655360 | tf_op jit(solution)/shard_map/all_gather | solution.py:127
  587.8 10.1 %reduce-scatter.9.cloned.1.call-done = bf16[2,2,1024,352]{2,3,0,1:T(8,128)(2,1)} async-done(((bf16[2,2,2048,352]{2,3,0,1:T(8,128)(2,1)}), bf16[2,2,1024,352]{2,3,0,1:T(8,128)(2,1)}) %reduce-scatter.9.cloned.1.call-update) | async-done | bytes 2883600 | tf_op jit(solution)/shard_map/reduce_scatter | solution.py:134
  601.6 44.2 %reduce-scatter.11.cloned.1.call-done = bf16[2,352,1024]{2,1,0:T(8,128)(2,1)} async-done(((bf16[2,352,2048]{2,1,0:T(8,128)(2,1)}), bf16[2,352,1024]{2,1,0:T(8,128)(2,1)}) %reduce-scatter.11.cloned.1.call-update) | async-done | bytes 1441808 | tf_op jit(solution)/shard_map/reduce_scatter | solution.py:137
  (107 shorter events, 99.4 us)
Async XLA Ops:
  8.0 1.6 copy-start
  8.0 53.9 %all-reduce.5.cloned.1.call-start = ((), (), s32[]{:S(2)}) async-start(), calls=%async_computation.8 | async-start | bytes 1048576 | tf_op jit(solution)/shard_map/psum | solution.py:49
  11.8 86.9 %all-gather.3.cloned.1.call-start = ((), (), s32[]{:S(2)}) async-start(), calls=%async_computation.9 | async-start | bytes 8650752 | tf_op jit(solution)/shard_map/all_gather | solution.py:45
  15.5 46.4 %copy-start.5 = (bf16[128,2048]{1,0:T(8,128)(2,1)S(1)}, bf16[128,2048]{1,0:T(8,128)(2,1)}, u32[]{:S(2)}) copy-start(bf16[128,2048]{1,0:T(8,128)(2,1)} %param.10) | copy-start | bytes 1572868
  15.5 47.7 %copy-start.11 = (f32[2048]{0:T(1024)S(1)}, f32[2048]{0:T(1024)}, u32[]{:S(2)}) copy-start(f32[2048]{0:T(1024)} %param.12) | copy-start | bytes 24580
  84.3 124.2 %all-to-all-start = ((bf16[2,32,14,2048]{3,0,2,1:T(2,128)(2,1)}), bf16[2,32,14,2048]{3,0,2,1:T(2,128)(2,1)}, u32[]{:S(2)}, u32[]{:S(2)}) async-start(bf16[2,32,14,2048]{3,0,2,1:T(2,128)(2,1)} %copy.53), calls=%async_computation | async-start | bytes 7340032 | tf_op jit(solution)/shard_map/all_to_all | solution.py:13
  96.8 128.1 %all-gather.5.cloned.1.call-start = ((), (), s32[]{:S(2)}) async-start(), calls=%async_computation.10 | async-start | bytes 4325376 | tf_op jit(solution)/shard_map/all_gather | solution.py:46
  97.3 174.9 %reduce-scatter.5.cloned.1.call-start = ((), (), s32[]{:S(2)}) async-start(), calls=%async_computation.11 | async-start | bytes 4587520 | tf_op jit(solution)/shard_map/reduce_scatter | solution.py:79
  208.5 8.6 %copy-start.1 = (bf16[2,2,2048,352]{2,3,0,1:T(8,128)(2,1)S(1)}, bf16[2,2,2048,352]{2,3,0,1:T(8,128)(2,1)}, u32[]{:S(2)}) copy-start(bf16[2,2,2048,352]{2,3,0,1:T(8,128)(2,1)} %all-gather.3.cloned.1.call-done) | copy-start | bytes 17301508
  224.8 5.9 copy-start.6
  230.8 55.3 %copy-start.13 = (f32[128,6]{0,1:T(8,128)S(1)}, f32[128,6]{0,1:T(8,128)}, u32[]{:S(2)}) copy-start(f32[128,6]{0,1:T(8,128)} %param.14) | copy-start | bytes 9220
  275.2 36.5 %all-to-all-start.1 = ((bf16[2,32,14,512]{3,0,2,1:T(2,128)(2,1)}), bf16[2,32,14,512]{3,0,2,1:T(2,128)(2,1)S(1)}, u32[]{:S(2)}, u32[]{:S(2)}) async-start(bf16[2,32,14,512]{3,0,2,1:T(2,128)(2,1)} %copy.57), calls=%async_computation.2 | async-start | bytes 1835008 | tf_op jit(solution)/shard_map/all_to_all | solution.py:17
  286.0 213.7 %reduce-scatter.7.cloned.1.call-start = ((), (), s32[]{:S(2)}) async-start(), calls=%async_computation.12 | async-start | bytes 4587520 | tf_op jit(solution)/shard_map/reduce_scatter | solution.py:109
  317.7 4.8 copy-start.10
  353.5 92.5 %copy-start.4 = (bf16[2,352,2048]{2,1,0:T(8,128)(2,1)S(1)}, bf16[2,352,2048]{2,1,0:T(8,128)(2,1)}, u32[]{:S(2)}) copy-start(bf16[2,352,2048]{2,1,0:T(8,128)(2,1)} %all-gather.5.cloned.1.call-done) | copy-start | bytes 8650756
  353.5 100.4 %slice-start = ((s8[5767168]{0:T(1024)(128)(4,1)}), s8[4194304]{0:T(1024)(128)(4,1)S(1)}, s32[]{:S(2)}) async-start(s8[5767168]{0:T(1024)(128)(4,1)} %bitcast.73), calls=%async_computation.15 | async-start | bytes 8388608
  446.0 7.9 %copy-start.2 = (bf16[2,32,14,2048]{3,0,2,1:T(2,128)(2,1)}, bf16[2,32,14,2048]{3,0,2,1:T(2,128)(2,1)S(1)}, u32[]{:S(2)}) copy-start(bf16[2,32,14,2048]{3,0,2,1:T(2,128)(2,1)S(1)} %all_to_all.20) | copy-start | bytes 11010052
  446.0 7.9 %slice-start.1 = ((s8[5767168]{0:T(1024)(128)(4,1)}), s8[1572864]{0:T(1024)(128)(4,1)S(1)}, s32[]{:S(2)}) async-start(s8[5767168]{0:T(1024)(128)(4,1)} %bitcast.73), calls=%async_computation.16 | async-start | bytes 3145728
  453.9 2.1 copy-start.8
  460.1 137.8 %reduce-scatter.9.cloned.1.call-start = ((), (), s32[]{:S(2)}) async-start(), calls=%async_computation.13 | async-start | bytes 8650752 | tf_op jit(solution)/shard_map/reduce_scatter | solution.py:134
  460.3 6.8 %copy-start.9 = (bf16[2,32,14,352]{3,1,2,0:T(8,128)(2,1)S(1)}, bf16[2,32,14,352]{3,1,2,0:T(8,128)(2,1)}, u32[]{:S(2)}) copy-start(bf16[2,32,14,352]{3,1,2,0:T(8,128)(2,1)} %copy-done.8) | copy-start | bytes 1892356
  477.0 168.7 %reduce-scatter.11.cloned.1.call-start = ((), (), s32[]{:S(2)}) async-start(), calls=%async_computation.14 | async-start | bytes 4325376 | tf_op jit(solution)/shard_map/reduce_scatter | solution.py:137
  502.8 46.7 %all-to-all-start.3 = ((bf16[2,32,14,512]{3,0,2,1:T(2,128)(2,1)}), bf16[2,32,14,512]{3,0,2,1:T(2,128)(2,1)S(1)}, u32[]{:S(2)}, u32[]{:S(2)}) async-start(bf16[2,32,14,512]{3,0,2,1:T(2,128)(2,1)} %copy.62), calls=%async_computation.5 | async-start | bytes 1835008 | tf_op jit(solution)/shard_map/all_to_all | solution.py:17
  555.5 5.0 copy-start.3
  (3 other events, 3.0 us)
Sparse Core Ops, SparseCore 0:
  11.9 49.9 all-reduce.4
  230.9 41.2 reduce-scatter.4
  460.2 39.4 reduce-scatter.6
  502.1 95.7 reduce-scatter.8
  600.8 44.8 reduce-scatter.10
Sparse Core Ops, SparseCore 1:
  15.6 83.0 all-gather.2
  100.3 108.2 all-gather.4
where the time goes:
time: 661 us; the launch traced here: 653 us
  waiting for transfers between devices  315 us (48%)
  blocking collectives  126 us (19%)
  local copies, waits for them, and re-layouts  78.2 us (12%)
  matrix products  60.6 us (9%)
  starting transfers between devices  34.5 us (5%)
  other arithmetic  22.9 us (3%)
  between operations  16.1 us (2%)
    all_to_all x1, waiting for transfers between devices, to_experts(): lax.all_to_all(outgoing, 'expert', split_axis=1, concat_axis=1, tiled=True)  110 us
    all_to_all x1, blocking collectives, to_experts(): lax.all_to_all(outgoing, 'expert', split_axis=1, concat_axis=1, tiled=True)  92.5 us
    all_to_all x2, waiting for transfers between devices, to_tokens(): lax.all_to_all(outgoing, 'expert', split_axis=1, concat_axis=1, tiled=True)  54.9 us
    reduce_scatter x1, waiting for transfers between devices, per_device(): lax.psum_scatter(down_part.astype(jnp.bfloat16), 'dp', scatter_dimension=...  44.2 us
    reduce_scatter x1, waiting for transfers between devices, per_device(): lax.psum_scatter(partial_out.astype(jnp.bfloat16), 'tensor', scatter_dime...  41.4 us
    psum x1, waiting for transfers between devices, per_device(): lax.psum(partial_attn.astype(jnp.bfloat16), 'tensor').astype(jnp.float32)  39.6 us
    all_to_all x2, starting transfers between devices, to_tokens(): lax.all_to_all(outgoing, 'expert', split_axis=1, concat_axis=1, tiled=True)  21.1 us
    reshape x2, local copies, waits for them, and re-layouts, per_device(): normed_pad[row_token]  13.8 us
  transfers between devices with their start and end apart: 10, of which 9 were waited for; matrix products, arithmetic and copies ran while one was open for 15% of the time, Pallas kernels for 0%

commit v1 on v0

--- a/solution.py
+++ b/solution.py
@@ -46,8 +46,8 @@
         lax.all_gather(w_down, "dp", axis=2, tiled=True),
     )
     partial_attn = jnp.dot(context, wo_rows, preferred_element_type=jnp.float32)
-    hidden_in = residual.astype(jnp.float32) + lax.psum(
-        partial_attn.astype(jnp.bfloat16), "tensor"
+    hidden_in = residual.astype(jnp.float32) + jnp.sum(
+        lax.all_gather(partial_attn.astype(jnp.bfloat16), "tensor"), axis=0
     ).astype(jnp.float32)
     inv_rms = lax.rsqrt(jnp.mean(hidden_in * hidden_in, axis=1, keepdims=True) + NORM_EPS)
     normed = (norm_gain * hidden_in * inv_rms).astype(jnp.bfloat16)

time: 661 us -> 699 us (1.057)
  waiting for transfers between devices: 315 us -> 355 us
    all_gather x1, waiting for transfers between devices: 1.05 us -> 126 us  [per_device(): lax.all_gather(w_gate_up, 'dp', axis=2, tiled=True)]
    all_to_all x1, waiting for transfers between devices: 110 us -> 0.01 us  [to_experts(): lax.all_to_all(outgoing, 'expert', split_axis=1, concat_axis=1, tiled=True)]
    psum x1 -> x0, waiting for transfers between devices: 39.6 us -> none  [per_device(): lax.psum(partial_attn.astype(jnp.bfloat16), 'tensor').astype(jnp.float32)]
    all_gather x1, waiting for transfers between devices: 0.01 us -> 33 us  [per_device(): lax.all_gather(w_down, 'dp', axis=2, tiled=True)]
    all_gather x0 -> x1, waiting for transfers between devices: none -> 26.5 us  [per_device(): lax.all_gather(partial_attn.astype(jnp.bfloat16), 'tensor')]
where the time goes in v1:
time: 699 us; the launch traced here: 690 us
  waiting for transfers between devices  355 us (51%)
  blocking collectives  126 us (18%)
  local copies, waits for them, and re-layouts  78.9 us (11%)
  matrix products  60.4 us (9%)
  starting transfers between devices  32.6 us (5%)
  other arithmetic  22.9 us (3%)
  between operations  15 us (2%)
    all_gather x1, waiting for transfers between devices, per_device(): lax.all_gather(w_gate_up, 'dp', axis=2, tiled=True)  126 us
    all_to_all x1, blocking collectives, to_experts(): lax.all_to_all(outgoing, 'expert', split_axis=1, concat_axis=1, tiled=True)  92.4 us
    all_to_all x2, waiting for transfers between devices, to_tokens(): lax.all_to_all(outgoing, 'expert', split_axis=1, concat_axis=1, tiled=True)  54.9 us
    reduce_scatter x1, waiting for transfers between devices, per_device(): lax.psum_scatter(partial_out.astype(jnp.bfloat16), 'tensor', scatter_dime...  45.7 us
    reduce_scatter x1, waiting for transfers between devices, per_device(): lax.psum_scatter(down_part.astype(jnp.bfloat16), 'dp', scatter_dimension=...  44.3 us
    all_gather x1, waiting for transfers between devices, per_device(): lax.all_gather(w_down, 'dp', axis=2, tiled=True)  33 us
    all_gather x1, waiting for transfers between devices, per_device(): lax.all_gather(partial_attn.astype(jnp.bfloat16), 'tensor')  26.5 us
    all_to_all x2, starting transfers between devices, to_tokens(): lax.all_to_all(outgoing, 'expert', split_axis=1, concat_axis=1, tiled=True)  21.1 us
  transfers between devices with their start and end apart: 10, of which 9 were waited for; matrix products, arithmetic and copies ran while one was open for 15% of the time, Pallas kernels for 0%

profile of v1, /device:TPU:1, one launch (start us, length us, event | category | flops | bytes accessed | tf_op | source)
XLA Modules:
  0.0 690.5 jit_solution(4348022232496850999)
XLA Ops:
  21.5 26.5 %all-gather.9.cloned.1.call-done = bf16[512,2048]{1,0:T(8,128)(2,1)} async-done(((bf16[128,2048]{1,0:T(8,128)(2,1)}), bf16[512,2048]{1,0:T(8,128)(2,1)}) %all-gather.9.cloned.1.call-update) | async-done | bytes 2097168 | tf_op jit(solution)/shard_map/all_gather | solution.py:50
  62.6 8.5 %copy.53 = bf16[2,32,14,2048]{3,0,2,1:T(2,128)(2,1)} copy(bf16[2,32,14,2048]{3,2,1,0:T(8,128)(2,1)} %reshape.133) | data formatting | bytes 7340032 | tf_op jit(solution)/shard_map/reshape | solution.py:69
  71.1 10.5 %all-to-all-start = ((bf16[2,32,14,2048]{3,0,2,1:T(2,128)(2,1)}), bf16[2,32,14,2048]{3,0,2,1:T(2,128)(2,1)}, u32[]{:S(2)}, u32[]{:S(2)}) async-start(bf16[2,32,14,2048]{3,0,2,1:T(2,128)(2,1)} %copy.53), calls=%async_computation | async-start | bytes 7340032 | tf_op jit(solution)/shard_map/all_to_all | solution.py:13
  82.6 126.1 %all-gather.5.cloned.1.call-done = bf16[2,2,2048,352]{2,3,0,1:T(8,128)(2,1)} async-done(((bf16[2,2,1024,352]{2,3,0,1:T(8,128)(2,1)}), bf16[2,2,2048,352]{2,3,0,1:T(8,128)(2,1)}) %all-gather.5.cloned.1.call-update) | async-done | bytes 5767184 | tf_op jit(solution)/shard_map/all_gather | solution.py:45
  208.7 7.4 %fusion.8 = f32[2,32,14,352]{3,1,2,0:T(8,128)S(1)} fusion(bf16[2,2,2048,352]{2,3,0,1:T(8,128)(2,1)} %all-gather.5.cloned.1.call-done, bf16[2,32,14,2048]{3,0,2,1:T(2,128)(2,1)} %all-to-all-done), kind=kOutput, calls=%fused_computation.23 | convolution fusion | flops 1291845632 | bytes 7815168 | tf_op jit(solution)/shard_map/escd,edf->escf/dot_general | solution.py:73
  217.3 7.7 %multiply_convert_fusion.3 = (bf16[2,32,14,352]{3,1,2,0:T(8,128)(2,1)S(1)}, f32[2,32,14,352]{3,1,2,0:T(8,128)}) fusion(f32[2,32,14,352]{3,1,2,0:T(8,128)S(1)} %fusion.8, bf16[2,2,2048,352]{2,3,0,1:T(8,128)(2,1)S(1)} %copy-done.1, bf16[2,32,14,2048]{3,0,2,1:T(2,128)(2,1)} %all-to-all-done), kind=kOutput, calls=%fused_computation.34 | convolution fusion | flops 1293737984 | bytes 9822208 | tf_op jit(solution)/shard_map/escd,edf->escf/dot_general | solution.py:74
  225.1 33.0 %all-gather.7.cloned.1.call-done = bf16[2,352,2048]{2,1,0:T(8,128)(2,1)} async-done(((bf16[2,352,1024]{2,1,0:T(8,128)(2,1)}), bf16[2,352,2048]{2,1,0:T(8,128)(2,1)}) %all-gather.7.cloned.1.call-update) | async-done | bytes 2883600 | tf_op jit(solution)/shard_map/all_gather | solution.py:46
  263.8 45.7 %reduce-scatter.5.cloned.1.call-done = bf16[2,32,14,512]{3,1,2,0:T(8,128)(2,1)} async-done(((bf16[2,32,14,2048]{3,1,2,0:T(8,128)(2,1)}), bf16[2,32,14,512]{3,1,2,0:T(8,128)(2,1)}) %reduce-scatter.5.cloned.1.call-update) | async-done | bytes 917520 | tf_op jit(solution)/shard_map/reduce_scatter | solution.py:79
  312.6 10.7 %all-to-all-start.1 = ((bf16[2,32,14,512]{3,0,2,1:T(2,128)(2,1)}), bf16[2,32,14,512]{3,0,2,1:T(2,128)(2,1)S(1)}, u32[]{:S(2)}, u32[]{:S(2)}) async-start(bf16[2,32,14,512]{3,0,2,1:T(2,128)(2,1)} %copy.57), calls=%async_computation.2 | async-start | bytes 1835008 | tf_op jit(solution)/shard_map/all_to_all | solution.py:17
  327.5 21.7 %all-to-all-done.1 = bf16[2,32,14,512]{3,0,2,1:T(2,128)(2,1)S(1)} async-done(((bf16[2,32,14,512]{3,0,2,1:T(2,128)(2,1)}), bf16[2,32,14,512]{3,0,2,1:T(2,128)(2,1)S(1)}, u32[]{:S(2)}, u32[]{:S(2)}) %all-to-all-start.1) | async-done | bytes 917536 | tf_op jit(solution)/shard_map/all_to_all | solution.py:17
  361.5 10.3 %all_gather.22 = bf16[128,2048]{1,0:T(8,128)(2,1)S(1)} all-gather(bf16[128,512]{1,0:T(8,128)(2,1)S(1)} %get-tuple-element.30), channel_id=1, replica_groups=mesh['dp'=2,'expert'=32,'tensor'=4] {'tensor'}, dimensions={1}, use_global_device_ids=true | all-gather | bytes 655360 | tf_op jit(solution)/shard_map/all_gather | solution.py:92
  376.8 6.3 reshape.138
  390.9 92.4 %all_to_all.20 = bf16[2,32,14,2048]{3,0,2,1:T(2,128)(2,1)S(1)} all-to-all(bf16[2,32,14,2048]{3,0,2,1:T(2,128)(2,1)S(1)} %copy.60), channel_id=1, replica_groups=mesh['dp'=2,'expert'=32,'tensor'=4] {'expert'}, dimensions={1} | all-to-all | bytes 7340032 | tf_op jit(solution)/shard_map/all_to_all | solution.py:13
  483.3 7.9 %multiply_convert_fusion.1 = (bf16[2,32,14,352]{3,1,2,0:T(8,128)(2,1)S(1)}, bf16[2,32,14,352]{3,1,2,0:T(8,128)(2,1)S(1)}) fusion(f32[2,32,14,352]{3,1,2,0:T(8,128)} %copy-done.14, f32[2,32,14,352]{3,1,2,0:T(8,128)} %get-tuple-element.41, bf16[2,352,2048]{2,1,0:T(8,128)(2,1)S(1)} %copy-done.4, bf16[2,32,14,2048]{3,0,2,1:T(2,128)(2,1)S(1)} %all_to_all.20), kind=kOutput, calls=%fused_computation.32 | convolution fusion | flops 1295945728 | bytes 10338304 | tf_op jit(solution)/shard_map/escd,efd->escf/dot_general | solution.py:97
  497.6 6.8 fusion.4
  504.5 6.8 fusion.3
  515.4 8.3 %bitcast_convert_fusion = bf16[2,352,2048]{2,1,0:T(8,128)(2,1)} fusion(bf16[2,32,14,352]{3,1,2,0:T(8,128)(2,1)S(1)} %copy-done.7, bf16[2,32,14,2048]{3,0,2,1:T(2,128)(2,1)} %copy-done.2), kind=kOutput, calls=%fused_computation.9 | convolution fusion | flops 1293287424 | bytes 7184384 | tf_op jit(solution)/shard_map/escf,escd->efd/dot_general | solution.py:21
  523.7 13.3 %reduce-scatter.7.cloned.1.call-done = bf16[2,32,14,512]{3,1,2,0:T(8,128)(2,1)} async-done(((bf16[2,32,14,2048]{3,1,2,0:T(8,128)(2,1)}), bf16[2,32,14,512]{3,1,2,0:T(8,128)(2,1)}) %reduce-scatter.7.cloned.1.call-update) | async-done | bytes 917520 | tf_op jit(solution)/shard_map/reduce_scatter | solution.py:109
  540.1 10.3 %all-to-all-start.3 = ((bf16[2,32,14,512]{3,0,2,1:T(2,128)(2,1)}), bf16[2,32,14,512]{3,0,2,1:T(2,128)(2,1)S(1)}, u32[]{:S(2)}, u32[]{:S(2)}) async-start(bf16[2,32,14,512]{3,0,2,1:T(2,128)(2,1)} %copy.62), calls=%async_computation.5 | async-start | bytes 1835008 | tf_op jit(solution)/shard_map/all_to_all | solution.py:17
  553.6 33.2 %all-to-all-done.3 = bf16[2,32,14,512]{3,0,2,1:T(2,128)(2,1)S(1)} async-done(((bf16[2,32,14,512]{3,0,2,1:T(2,128)(2,1)}), bf16[2,32,14,512]{3,0,2,1:T(2,128)(2,1)S(1)}, u32[]{:S(2)}, u32[]{:S(2)}) %all-to-all-start.3) | async-done | bytes 917536 | tf_op jit(solution)/shard_map/all_to_all | solution.py:17
  598.0 12.6 %all-reduce.2 = (f32[128]{0:T(128)}, f32[128,6]{1,0:T(8,128)}) all-reduce(f32[128]{0:T(128)S(1)} %multiply_reduce_fusion.3, f32[128,6]{1,0:T(8,128)} %multiply_reduce_fusion), channel_id=1, replica_groups=mesh['dp'=2,'expert'=32,'tensor'=4] {'tensor'}, use_global_device_ids=true, to_apply=%region_12.13 | all-reduce | flops 896 | bytes 7168 | tf_op jit(solution)/shard_map/psum | solution.py:119
  612.9 10.6 %all_gather.23 = bf16[128,2048]{1,0:T(8,128)(2,1)S(1)} all-gather(bf16[128,512]{1,0:T(8,128)(2,1)S(1)} %subtract_convert_fusion), channel_id=1, replica_groups=mesh['dp'=2,'expert'=32,'tensor'=4] {'tensor'}, dimensions={1}, use_global_device_ids=true | all-gather | bytes 655360 | tf_op jit(solution)/shard_map/all_gather | solution.py:127
  625.0 10.1 %reduce-scatter.9.cloned.1.call-done = bf16[2,2,1024,352]{2,3,0,1:T(8,128)(2,1)} async-done(((bf16[2,2,2048,352]{2,3,0,1:T(8,128)(2,1)}), bf16[2,2,1024,352]{2,3,0,1:T(8,128)(2,1)}) %reduce-scatter.9.cloned.1.call-update) | async-done | bytes 2883600 | tf_op jit(solution)/shard_map/reduce_scatter | solution.py:134
  638.8 44.3 %reduce-scatter.11.cloned.1.call-done = bf16[2,352,1024]{2,1,0:T(8,128)(2,1)} async-done(((bf16[2,352,2048]{2,1,0:T(8,128)(2,1)}), bf16[2,352,1024]{2,1,0:T(8,128)(2,1)}) %reduce-scatter.11.cloned.1.call-update) | async-done | bytes 1441808 | tf_op jit(solution)/shard_map/reduce_scatter | solution.py:137
  (108 shorter events, 104.1 us)
Async XLA Ops:
  7.2 1.6 copy-start
  7.2 40.8 %all-gather.9.cloned.1.call-start = ((), (), s32[]{:S(2)}) async-start(), calls=%async_computation.14 | async-start | bytes 2621440 | tf_op jit(solution)/shard_map/all_gather | solution.py:50
  10.9 197.8 %all-gather.5.cloned.1.call-start = ((), (), s32[]{:S(2)}) async-start(), calls=%async_computation.8 | async-start | bytes 8650752 | tf_op jit(solution)/shard_map/all_gather | solution.py:45
  14.7 35.4 %copy-start.5 = (bf16[128,2048]{1,0:T(8,128)(2,1)S(1)}, bf16[128,2048]{1,0:T(8,128)(2,1)}, u32[]{:S(2)}) copy-start(bf16[128,2048]{1,0:T(8,128)(2,1)} %param.10) | copy-start | bytes 1572868
  14.7 35.6 %copy-start.11 = (f32[2048]{0:T(1024)S(1)}, f32[2048]{0:T(1024)}, u32[]{:S(2)}) copy-start(f32[2048]{0:T(1024)} %param.12) | copy-start | bytes 24580
  71.1 137.7 %all-to-all-start = ((bf16[2,32,14,2048]{3,0,2,1:T(2,128)(2,1)}), bf16[2,32,14,2048]{3,0,2,1:T(2,128)(2,1)}, u32[]{:S(2)}, u32[]{:S(2)}) async-start(bf16[2,32,14,2048]{3,0,2,1:T(2,128)(2,1)} %copy.53), calls=%async_computation | async-start | bytes 7340032 | tf_op jit(solution)/shard_map/all_to_all | solution.py:13
  81.6 176.5 %all-gather.7.cloned.1.call-start = ((), (), s32[]{:S(2)}) async-start(), calls=%async_computation.9 | async-start | bytes 4325376 | tf_op jit(solution)/shard_map/all_gather | solution.py:46
  82.3 227.2 %reduce-scatter.5.cloned.1.call-start = ((), (), s32[]{:S(2)}) async-start(), calls=%async_computation.10 | async-start | bytes 4587520 | tf_op jit(solution)/shard_map/reduce_scatter | solution.py:79
  208.7 8.6 %copy-start.1 = (bf16[2,2,2048,352]{2,3,0,1:T(8,128)(2,1)S(1)}, bf16[2,2,2048,352]{2,3,0,1:T(8,128)(2,1)}, u32[]{:S(2)}) copy-start(bf16[2,2,2048,352]{2,3,0,1:T(8,128)(2,1)} %all-gather.5.cloned.1.call-done) | copy-start | bytes 17301508
  225.1 38.7 %copy-start.6 = (bf16[2,32,14,352]{3,1,2,0:T(8,128)(2,1)}, bf16[2,32,14,352]{3,1,2,0:T(8,128)(2,1)S(1)}, u32[]{:S(2)}) copy-start(bf16[2,32,14,352]{3,1,2,0:T(8,128)(2,1)S(1)} %get-tuple-element.40) | copy-start | bytes 1892356
  263.7 59.6 %copy-start.13 = (f32[128,6]{0,1:T(8,128)S(1)}, f32[128,6]{0,1:T(8,128)}, u32[]{:S(2)}) copy-start(f32[128,6]{0,1:T(8,128)} %param.14) | copy-start | bytes 9220
  312.6 36.6 %all-to-all-start.1 = ((bf16[2,32,14,512]{3,0,2,1:T(2,128)(2,1)}), bf16[2,32,14,512]{3,0,2,1:T(2,128)(2,1)S(1)}, u32[]{:S(2)}, u32[]{:S(2)}) async-start(bf16[2,32,14,512]{3,0,2,1:T(2,128)(2,1)} %copy.57), calls=%async_computation.2 | async-start | bytes 1835008 | tf_op jit(solution)/shard_map/all_to_all | solution.py:17
  323.3 213.7 %reduce-scatter.7.cloned.1.call-start = ((), (), s32[]{:S(2)}) async-start(), calls=%async_computation.11 | async-start | bytes 4587520 | tf_op jit(solution)/shard_map/reduce_scatter | solution.py:109
  355.0 4.8 copy-start.10
  390.8 92.5 %copy-start.4 = (bf16[2,352,2048]{2,1,0:T(8,128)(2,1)S(1)}, bf16[2,352,2048]{2,1,0:T(8,128)(2,1)}, u32[]{:S(2)}) copy-start(bf16[2,352,2048]{2,1,0:T(8,128)(2,1)} %all-gather.7.cloned.1.call-done) | copy-start | bytes 8650756
  390.8 100.4 %slice-start = ((s8[5767168]{0:T(1024)(128)(4,1)}), s8[4194304]{0:T(1024)(128)(4,1)S(1)}, s32[]{:S(2)}) async-start(s8[5767168]{0:T(1024)(128)(4,1)} %bitcast.74), calls=%async_computation.15 | async-start | bytes 8388608
  483.3 7.9 %copy-start.2 = (bf16[2,32,14,2048]{3,0,2,1:T(2,128)(2,1)}, bf16[2,32,14,2048]{3,0,2,1:T(2,128)(2,1)S(1)}, u32[]{:S(2)}) copy-start(bf16[2,32,14,2048]{3,0,2,1:T(2,128)(2,1)S(1)} %all_to_all.20) | copy-start | bytes 11010052
  483.3 7.9 %slice-start.1 = ((s8[5767168]{0:T(1024)(128)(4,1)}), s8[1572864]{0:T(1024)(128)(4,1)S(1)}, s32[]{:S(2)}) async-start(s8[5767168]{0:T(1024)(128)(4,1)} %bitcast.74), calls=%async_computation.16 | async-start | bytes 3145728
  491.2 2.1 copy-start.8
  497.4 137.8 %reduce-scatter.9.cloned.1.call-start = ((), (), s32[]{:S(2)}) async-start(), calls=%async_computation.12 | async-start | bytes 8650752 | tf_op jit(solution)/shard_map/reduce_scatter | solution.py:134
  497.6 6.8 copy-start.9
  514.3 168.9 %reduce-scatter.11.cloned.1.call-start = ((), (), s32[]{:S(2)}) async-start(), calls=%async_computation.13 | async-start | bytes 4325376 | tf_op jit(solution)/shard_map/reduce_scatter | solution.py:137
  540.1 46.7 %all-to-all-start.3 = ((bf16[2,32,14,512]{3,0,2,1:T(2,128)(2,1)}), bf16[2,32,14,512]{3,0,2,1:T(2,128)(2,1)S(1)}, u32[]{:S(2)}, u32[]{:S(2)}) async-start(bf16[2,32,14,512]{3,0,2,1:T(2,128)(2,1)} %copy.62), calls=%async_computation.5 | async-start | bytes 1835008 | tf_op jit(solution)/shard_map/all_to_all | solution.py:17
  592.8 5.0 copy-start.3
  (3 other events, 3.0 us)
Sparse Core Ops, SparseCore 0:
  11.1 36.9 all-gather.8
  50.4 158.2 all-gather.4
  210.5 47.4 all-gather.6
  263.9 45.5 reduce-scatter.4
  497.5 39.4 reduce-scatter.6
  539.4 95.7 reduce-scatter.8
  638.3 44.8 reduce-scatter.10
